TPU v7x, 512 devices: a whole 4x4x16 slice. The times are simulated.
512 devices in a mesh: seg: 64 (over y, z_lo, core), blk: 8 (over x, z_hi).
Axes of the slice: x: 4, y: 4, z: 16 (z_hi: 2, z_lo: 8; z = z_hi * 8 + z_lo), core: 2. Of those that a mesh axis runs over, the one named last changes fastest.
Arguments:
- record: float32 [24, 262144], P(None, ('seg', 'blk')), may hold values from -8 to 8, as said below
- templates: bfloat16 [128, 24, 512], P('blk'), may hold values from -6 to 6
Outputs:
- detection: float32 [128, 262144], P(None, ('seg', 'blk'))
Inputs may be any that keep to these rules, and one draw needn't show every extreme that they name: `record`: network samples.
All inputs are finite; a program needn't handle non-finite values.
Results may differ from a plain program's by a relative error of at most 0.0032.
Values may be sent and summed in bfloat16 or wider, within the bound.
No kernel may reach another device: no remote copies, remote signals or barrier semaphores. Data moves between devices by JAX's collectives and lax.ppermute only.
A program may use at most 64 MiB of HBM per device.

v0:
```python
import jax
import jax.numpy as jnp
from jax import lax
from jax.sharding import PartitionSpec as P


def passed_along(block, axis, distance):
    devices = range(lax.axis_size(axis))
    route = [(i - distance, i) for i in devices if i - distance in devices]
    return lax.ppermute(block, axis, route)


def normalize(templates):
    widened = templates.astype(jnp.float32)
    centred = widened - jnp.mean(widened, axis=2, keepdims=True)
    return (centred / jnp.sqrt(jnp.sum(centred * centred, axis=2, keepdims=True) + 1e-06)).astype(
        jnp.bfloat16
    )


def band_matrix(samples, window):
    span = samples + window - 1
    rows = jnp.arange(span, dtype=jnp.int32)[:, None]
    cols = jnp.arange(samples, dtype=jnp.int32)[None, :]
    inside = jnp.logical_and(rows >= cols, rows < cols + window)
    return inside.astype(jnp.float32)


def window_scale(extended, band, window):
    stacked_rows = jnp.concatenate([extended, extended * extended], axis=0)
    sums = jnp.dot(
        stacked_rows, band, precision=lax.Precision.HIGHEST, preferred_element_type=jnp.float32
    )
    channels = extended.shape[0]
    window_sum = sums[:channels]
    window_sq = sums[channels:]
    spread = window_sq - window_sum * window_sum / window
    return 1.0 / jnp.sqrt(jnp.maximum(spread, 1.0))


def correlate(record_bf, kernel_block, scale):
    members = kernel_block.shape[0]
    channels = kernel_block.shape[1]
    window = kernel_block.shape[2]
    samples = scale.shape[1]
    span = record_bf.shape[1]
    kernels = jnp.transpose(kernel_block, (1, 0, 2))

    def one_channel(total, inputs):
        channel_row, kernel_rows, factor = inputs
        repeated = jnp.tile(channel_row, window + 1)[: window * (span + 1)]
        hankel = repeated.reshape(window, span + 1)[:, :samples]
        product = jnp.dot(kernel_rows, hankel, preferred_element_type=jnp.float32)
        return (total + product * factor[None, :], None)

    total, unused = lax.scan(
        one_channel, jnp.zeros((members, samples), jnp.float32), (record_bf, kernels, scale)
    )
    return total / channels


def body(record, templates):
    samples = record.shape[1]
    window = templates.shape[2]
    trailing = passed_along(record, ("seg", "blk"), -1)
    padded_rec = jnp.concatenate([record, trailing], axis=1)
    normalized = normalize(templates)
    band = band_matrix(samples, window)
    extended = padded_rec[:, : samples + window - 1]
    scale = window_scale(extended, band, window)
    record_bf = extended.astype(jnp.bfloat16)
    collected = lax.all_gather(normalized, "blk", axis=0, tiled=True)
    stacked = correlate(record_bf, collected, scale)
    power_sum = lax.psum(jnp.sum(stacked * stacked, axis=1), ("seg", "blk"))
    record_len = samples * lax.axis_size("seg") * lax.axis_size("blk")
    return stacked / jnp.sqrt(power_sum / record_len + 1e-06)[:, None]


def solution(mesh):
    return jax.shard_map(
        body,
        mesh=mesh,
        in_specs=(P(None, ("seg", "blk")), P("blk", None, None)),
        out_specs=P(None, ("seg", "blk")),
        check_vma=False,
    )
```

profile of v0, /device:TPU:1, one launch (start us, length us, event | category | flops | bytes accessed | tf_op | source)
XLA Modules:
  0.0 357.7 jit_solution(17654023932856735463)
XLA Ops:
  9.0 1.9 fusion.12
  11.0 19.0 %collective-permute-start = (f32[24,512]{1,0:T(8,128)}, f32[24,512]{1,0:T(8,128)S(1)}, u32[]{:S(2)}, u32[]{:S(2)}) collective-permute-start(f32[24,512]{1,0:T(8,128)} %param.4), channel_id=1, source_target_pairs={{1,0},{2,1},{3,2},{4,3},{5,4},{6,5},{7,6},{8,7},{9,8},{10,9},{11,1... | collective-permute-start | bytes 147464 | tf_op jit(solution)/shard_map/ppermute | solution.py:10
  32.4 129.1 %all-gather.2.cloned.1.call-done = bf16[128,24,512]{2,0,1:T(8,128)(2,1)} async-done(((bf16[16,24,512]{2,0,1:T(8,128)(2,1)}), bf16[128,24,512]{2,0,1:T(8,128)(2,1)}) %all-gather.2.cloned.1.call-update) | async-done | bytes 3145744 | tf_op jit(solution)/shard_map/all_gather | solution.py:72
  161.6 86.4 %while.11 = (s32[]{:T(128)}, f32[128,512]{1,0:T(8,128)S(1)}, bf16[24,128,512]{2,1,0:T(8,128)(2,1)}, bf16[24,1023]{1,0:T(8,128)(2,1)S(1)}, f32[24,512]{1,0:T(8,128)S(1)}, /*index=5*/s32[]{:T(128)}, s32[]{:T(128)}) while((s32[]{:T(128)}, f32[128,512]{1,0:T(8,128)S(1)}, bf16[24,128,512]{2,1,0:T(8,128)(2,1)}, ...), condition=%wide.region_3.4_spmd.clone, body=%wide.region_2.3_spmd.clone.sunk | while | flops 67305472 | bytes 8535635 | solution.py:56
  161.7 1.6 tile.17
  165.3 1.6 tile.17
  168.9 1.6 tile.17
  172.5 1.6 tile.17
  176.1 1.6 tile.17
  179.7 1.6 tile.17
  183.3 1.6 tile.17
  186.9 1.6 tile.17
  190.5 1.6 tile.17
  194.1 1.6 tile.17
  197.7 1.6 tile.17
  201.3 1.6 tile.17
  204.9 1.6 tile.17
  208.5 1.6 tile.17
  212.1 1.6 tile.17
  219.3 1.6 tile.17
  226.5 1.6 tile.17
  233.7 1.6 tile.17
  240.9 1.6 tile.17
  248.1 102.0 %psum.7 = f32[128]{0:T(128)S(1)} all-reduce(f32[128]{0:T(128)S(1)} %multiply_reduce_fusion), channel_id=1, replica_groups=mesh['seg'=64,'blk'=8] {'seg','blk'}, use_global_device_ids=true, to_apply=%region_5.6 | all-reduce | flops 128 | bytes 1024 | tf_op jit(solution)/shard_map/psum | solution.py:74
  (167 shorter events, 59.5 us)
Async XLA Ops:
  6.5 25.0 %copy-start = (f32[24,512]{1,0:T(8,128)S(1)}, f32[24,512]{1,0:T(8,128)}, u32[]{:S(2)}) copy-start(f32[24,512]{1,0:T(8,128)} %param.4) | copy-start | bytes 147460
  6.5 155.0 %all-gather.2.cloned.1.call-start = ((), (), s32[]{:S(2)}) async-start(), calls=%async_computation | async-start | bytes 3538944 | tf_op jit(solution)/shard_map/all_gather | solution.py:72
  11.0 20.5 %collective-permute-start = (f32[24,512]{1,0:T(8,128)}, f32[24,512]{1,0:T(8,128)S(1)}, u32[]{:S(2)}, u32[]{:S(2)}) collective-permute-start(f32[24,512]{1,0:T(8,128)} %param.4), channel_id=1, source_target_pairs={{1,0},{2,1},{3,2},{4,3},{5,4},{6,5},{7,6},{8,7},{9,8},{10,9},{11,1... | collective-permute-start | bytes 147464 | tf_op jit(solution)/shard_map/ppermute | solution.py:10
Sparse Core Ops, SparseCore 0:
  11.1 150.3 all-gather.1
where the time goes:
time: 358 us
  waiting for transfers between devices  131 us (37%)
  blocking collectives  102 us (28%)
  local copies, waits for them, and re-layouts  56.6 us (16%)
  matrix products  29 us (8%)
  starting transfers between devices  19 us (5%)
  between operations  13.5 us (4%)
  other arithmetic  5.36 us (1%)
    all_gather x1, waiting for transfers between devices, body(): collected = lax.all_gather(normalized, 'blk', axis=0, tiled=True)  129 us
    psum x1, blocking collectives, body(): power_sum = lax.psum(jnp.sum(stacked * stacked, axis=1), ('seg', 'blk'))  102 us
    another operation x48, local copies, waits for them, and re-layouts, one_channel(): repeated = jnp.tile(channel_row, window + 1)[:window * (span + 1)]  42.1 us
    dot_general x24, matrix products, one_channel(): product = jnp.dot(kernel_rows, hankel, preferred_element_type=jnp.float32)  28.2 us
    ppermute x1, starting transfers between devices, passed_along(): return lax.ppermute(block, axis, route)  19 us
    reshape x24, local copies, waits for them, and re-layouts, one_channel(): hankel = repeated.reshape(window, span + 1)[:, :samples]  11.8 us
  transfers between devices with their start and end apart: 2, of which 2 were waited for; matrix products, arithmetic and copies ran while one was open for 0% of the time, Pallas kernels for 0%

commit v1 on v0

--- a/solution.py
+++ b/solution.py
@@ -2,6 +2,12 @@
 import jax.numpy as jnp
 from jax import lax
 from jax.sharding import PartitionSpec as P
+
+
+def gather_and_add(array, name):
+    parts = lax.all_gather(array, name, axis=0, tiled=False)
+    total = parts.sum(axis=0)
+    return total
 
 
 def passed_along(block, axis, distance):
@@ -71,7 +77,7 @@
     record_bf = extended.astype(jnp.bfloat16)
     collected = lax.all_gather(normalized, "blk", axis=0, tiled=True)
     stacked = correlate(record_bf, collected, scale)
-    power_sum = lax.psum(jnp.sum(stacked * stacked, axis=1), ("seg", "blk"))
+    power_sum = gather_and_add(jnp.sum(stacked * stacked, axis=1), ("seg", "blk"))
     record_len = samples * lax.axis_size("seg") * lax.axis_size("blk")
     return stacked / jnp.sqrt(power_sum / record_len + 1e-06)[:, None]
 

time: 358 us -> 2180 us (6.09)
  blocking collectives: 102 us -> 1930 us
    all_gather x0 -> x1, blocking collectives: none -> 1930 us  [gather_and_add(): parts = lax.all_gather(array, name, axis=0, tiled=False)]
    psum x1 -> x0, blocking collectives: 102 us -> none  [body(): power_sum = lax.psum(jnp.sum(stacked * stacked, axis=1), ('seg', 'blk'))]
where the time goes in v1:
time: 2180 us
  blocking collectives  1930 us (89%)
  waiting for transfers between devices  131 us (6%)
  local copies, waits for them, and re-layouts  56.6 us (3%)
  matrix products  29 us (1%)
    all_gather x1, blocking collectives, gather_and_add(): parts = lax.all_gather(array, name, axis=0, tiled=False)  1930 us
    all_gather x1, waiting for transfers between devices, body(): collected = lax.all_gather(normalized, 'blk', axis=0, tiled=True)  129 us
  transfers between devices with their start and end apart: 2, of which 2 were waited for; matrix products, arithmetic and copies ran while one was open for 0% of the time, Pallas kernels for 0%

profile of v1, /device:TPU:1, one launch (start us, length us, event | category | flops | bytes accessed | tf_op | source)
XLA Modules:
  0.0 2181.4 jit_solution(5423996162603695659)
XLA Ops:
  9.0 1.9 fusion.12
  11.0 19.0 collective-permute-start
  32.4 129.1 %all-gather.4.cloned.1.call-done = bf16[128,24,512]{2,0,1:T(8,128)(2,1)} async-done(((bf16[16,24,512]{2,0,1:T(8,128)(2,1)}), bf16[128,24,512]{2,0,1:T(8,128)(2,1)}) %all-gather.4.cloned.1.call-update) | async-done | bytes 3145744 | tf_op jit(solution)/shard_map/all_gather | solution.py:78
  161.6 86.4 %while.11 = (s32[]{:T(128)}, f32[128,512]{1,0:T(8,128)S(1)}, bf16[24,128,512]{2,1,0:T(8,128)(2,1)}, bf16[24,1023]{1,0:T(8,128)(2,1)S(1)}, f32[24,512]{1,0:T(8,128)S(1)}, /*index=5*/s32[]{:T(128)}, s32[]{:T(128)}) while((s32[]{:T(128)}, f32[128,512]{1,0:T(8,128)S(1)}, bf16[24,128,512]{2,1,0:T(8,128)(2,1)}, ...), condition=%wide.region_3.4_spmd.clone, body=%wide.region_2.3_spmd.clone.sunk | while | flops 67305472 | bytes 8535635 | solution.py:62
  161.7 1.6 tile.17
  165.3 1.6 tile.17
  168.9 1.6 tile.17
  172.5 1.6 tile.17
  176.1 1.6 tile.17
  179.7 1.6 tile.17
  183.3 1.6 tile.17
  186.9 1.6 tile.17
  190.5 1.6 tile.17
  194.1 1.6 tile.17
  197.7 1.6 tile.17
  201.3 1.6 tile.17
  204.9 1.6 tile.17
  208.5 1.6 tile.17
  212.1 1.6 tile.17
  219.3 1.6 tile.17
  226.5 1.6 tile.17
  233.7 1.6 tile.17
  240.9 1.6 tile.17
  248.1 1925.1 %all-gather.1 = f32[512,1,128]{2,1,0:T(1,128)S(1)} all-gather(f32[1,1,128]{2,1,0:T(1,128)S(1)} %bitcast.12), channel_id=2, replica_groups=mesh['seg'=64,'blk'=8] {'seg','blk'}, dimensions={0}, use_global_device_ids=true | all-gather | bytes 262656 | tf_op jit(solution)/shard_map/all_gather | solution.py:8
  (168 shorter events, 60.1 us)
Async XLA Ops:
  6.5 25.0 %copy-start = (f32[24,512]{1,0:T(8,128)S(1)}, f32[24,512]{1,0:T(8,128)}, u32[]{:S(2)}) copy-start(f32[24,512]{1,0:T(8,128)} %param.4) | copy-start | bytes 147460
  6.5 155.0 %all-gather.4.cloned.1.call-start = ((), (), s32[]{:S(2)}) async-start(), calls=%async_computation | async-start | bytes 3538944 | tf_op jit(solution)/shard_map/all_gather | solution.py:78
  11.0 20.5 collective-permute-start
Sparse Core Ops, SparseCore 0:
  11.1 150.3 all-gather.3

commit v2 on v0

--- a/solution.py
+++ b/solution.py
@@ -2,6 +2,13 @@
 import jax.numpy as jnp
 from jax import lax
 from jax.sharding import PartitionSpec as P
+from jax.lax import all_to_all, axis_size
+
+
+def produce_the_rings(z_in, on_dim):
+    return jnp.concatenate(
+        all_to_all(jnp.stack([z_in for _ in range(axis_size("blk"))], axis=0), "blk", 0, 0), on_dim
+    )
 
 
 def passed_along(block, axis, distance):
@@ -69,7 +76,7 @@
     extended = padded_rec[:, : samples + window - 1]
     scale = window_scale(extended, band, window)
     record_bf = extended.astype(jnp.bfloat16)
-    collected = lax.all_gather(normalized, "blk", axis=0, tiled=True)
+    collected = produce_the_rings(normalized, 0)
     stacked = correlate(record_bf, collected, scale)
     power_sum = lax.psum(jnp.sum(stacked * stacked, axis=1), ("seg", "blk"))
     record_len = samples * lax.axis_size("seg") * lax.axis_size("blk")

time: 358 us -> 372 us (1.039)
  blocking collectives: 102 us -> 182 us
  waiting for transfers between devices: 131 us -> 55.2 us
  starting transfers between devices: 19 us -> 33.5 us
  between operations: 13.5 us -> 0.11 us
  local copies, waits for them, and re-layouts: 56.6 us -> 65.3 us
    all_gather x1 -> x0, waiting for transfers between devices: 129 us -> none  [body(): collected = lax.all_gather(normalized, 'blk', axis=0, tiled=True)]
    psum x1, blocking collectives: 102 us -> 182 us  [body(): power_sum = lax.psum(jnp.sum(stacked * stacked, axis=1), ('seg', 'blk'))]
    ppermute x1, waiting for transfers between devices: 1.45 us -> 53.6 us  [passed_along(): return lax.ppermute(block, axis, route)]
    all_to_all x0 -> x1, starting transfers between devices: none -> 18.2 us  [produce_the_rings(): all_to_all(jnp.stack([z_in for _ in range(axis_size('blk'))], axis=0), 'b...]
    all_to_all x0 -> x1, local copies, waits for them, and re-layouts: none -> 3.77 us  [produce_the_rings(): all_to_all(jnp.stack([z_in for _ in range(axis_size('blk'))], axis=0), 'b...]
    ppermute x1, starting transfers between devices: 19 us -> 15.3 us  [passed_along(): return lax.ppermute(block, axis, route)]
where the time goes in v2:
time: 372 us; the launch traced here: 371 us
  blocking collectives  182 us (49%)
  local copies, waits for them, and re-layouts  65.3 us (18%)
  waiting for transfers between devices  55.2 us (15%)
  starting transfers between devices  33.5 us (9%)
  matrix products  29 us (8%)
  other arithmetic  4.51 us (1%)
    psum x1, blocking collectives, body(): power_sum = lax.psum(jnp.sum(stacked * stacked, axis=1), ('seg', 'blk'))  182 us
    ppermute x1, waiting for transfers between devices, passed_along(): return lax.ppermute(block, axis, route)  53.6 us
    another operation x48, local copies, waits for them, and re-layouts, one_channel(): repeated = jnp.tile(channel_row, window + 1)[:window * (span + 1)]  42.1 us
    dot_general x24, matrix products, one_channel(): product = jnp.dot(kernel_rows, hankel, preferred_element_type=jnp.float32)  28.2 us
    all_to_all x1, starting transfers between devices, produce_the_rings(): all_to_all(jnp.stack([z_in for _ in range(axis_size('blk'))], axis=0), 'b...  18.2 us
    ppermute x1, starting transfers between devices, passed_along(): return lax.ppermute(block, axis, route)  15.3 us
    reshape x24, local copies, waits for them, and re-layouts, one_channel(): hankel = repeated.reshape(window, span + 1)[:, :samples]  11.8 us
  transfers between devices with their start and end apart: 2, of which 2 were waited for; matrix products, arithmetic and copies ran while one was open for 0% of the time, Pallas kernels for 0%

profile of v2, /device:TPU:1, one launch (start us, length us, event | category | flops | bytes accessed | tf_op | source)
XLA Modules:
  0.0 371.0 jit_solution(13646311777862588413)
XLA Ops:
  3.7 2.1 stack.2
  5.8 18.2 %all-to-all-start = ((bf16[8,16,24,512]{3,1,2,0:T(8,128)(2,1)}), bf16[8,16,24,512]{3,1,2,0:T(8,128)(2,1)}, u32[]{:S(2)}, u32[]{:S(2)}) async-start(bf16[8,16,24,512]{3,1,2,0:T(8,128)(2,1)} %stack.2), calls=%async_computation | async-start | bytes 6291456 | tf_op jit(solution)/shard_map/all_to_all | solution.py:10
  24.1 15.3 %collective-permute-start = (f32[24,512]{1,0:T(8,128)S(1)}, f32[24,512]{1,0:T(8,128)S(1)}, u32[]{:S(2)}, u32[]{:S(2)}) collective-permute-start(f32[24,512]{1,0:T(8,128)S(1)} %copy-done), channel_id=1, source_target_pairs={{1,0},{2,1},{3,2},{4,3},{5,4},{6,5},{7,6},{8,7},{9,8},{10,9},{11,1... | collective-permute-start | bytes 147464 | tf_op jit(solution)/shard_map/ppermute | solution.py:17
  39.4 53.6 %collective-permute-done = f32[24,512]{1,0:T(8,128)S(1)} collective-permute-done((f32[24,512]{1,0:T(8,128)S(1)}, f32[24,512]{1,0:T(8,128)S(1)}, u32[]{:S(2)}, u32[]{:S(2)}) %collective-permute-start) | collective-permute-done | bytes 49184 | tf_op jit(solution)/shard_map/ppermute | solution.py:17
  95.5 3.8 %copy.6 = bf16[8,16,24,512]{3,2,1,0:T(8,128)(2,1)S(1)} copy(bf16[8,16,24,512]{3,1,2,0:T(8,128)(2,1)} %all-to-all-done) | data formatting | bytes 6291456 | tf_op jit(solution)/shard_map/all_to_all | solution.py:10
  99.3 2.7 copy.7
  102.0 86.4 %while.11 = (s32[]{:T(128)}, f32[128,512]{1,0:T(8,128)S(1)}, bf16[24,128,512]{2,1,0:T(8,128)(2,1)}, bf16[24,1023]{1,0:T(8,128)(2,1)S(1)}, f32[24,512]{1,0:T(8,128)S(1)}, /*index=5*/s32[]{:T(128)}, s32[]{:T(128)}) while((s32[]{:T(128)}, f32[128,512]{1,0:T(8,128)S(1)}, bf16[24,128,512]{2,1,0:T(8,128)(2,1)}, ...), condition=%wide.region_3.4_spmd.clone, body=%wide.region_2.3_spmd.clone.sunk | while | flops 67305472 | bytes 8535635 | solution.py:63
  102.2 1.6 tile.17
  105.8 1.6 tile.17
  109.4 1.6 tile.17
  113.0 1.6 tile.17
  123.8 1.6 tile.17
  127.4 1.6 tile.17
  131.0 1.6 tile.17
  134.6 1.6 tile.17
  138.2 1.6 tile.17
  141.8 1.6 tile.17
  145.4 1.6 tile.17
  149.0 1.6 tile.17
  152.6 1.6 tile.17
  156.2 1.6 tile.17
  159.8 1.6 tile.17
  163.4 1.6 tile.17
  188.5 181.7 %psum.7 = f32[128]{0:T(128)S(1)} all-reduce(f32[128]{0:T(128)S(1)} %multiply_reduce_fusion), channel_id=1, replica_groups=mesh['seg'=64,'blk'=8] {'seg','blk'}, use_global_device_ids=true, to_apply=%region_5.6 | all-reduce | flops 128 | bytes 1024 | tf_op jit(solution)/shard_map/psum | solution.py:81
  (170 shorter events, 65.7 us)
Async XLA Ops:
  5.8 18.2 %copy-start = (f32[24,512]{1,0:T(8,128)S(1)}, f32[24,512]{1,0:T(8,128)}, u32[]{:S(2)}) copy-start(f32[24,512]{1,0:T(8,128)} %param.4) | copy-start | bytes 147460
  5.8 89.7 %all-to-all-start = ((bf16[8,16,24,512]{3,1,2,0:T(8,128)(2,1)}), bf16[8,16,24,512]{3,1,2,0:T(8,128)(2,1)}, u32[]{:S(2)}, u32[]{:S(2)}) async-start(bf16[8,16,24,512]{3,1,2,0:T(8,128)(2,1)} %stack.2), calls=%async_computation | async-start | bytes 6291456 | tf_op jit(solution)/shard_map/all_to_all | solution.py:10
  24.1 69.0 %collective-permute-start = (f32[24,512]{1,0:T(8,128)S(1)}, f32[24,512]{1,0:T(8,128)S(1)}, u32[]{:S(2)}, u32[]{:S(2)}) collective-permute-start(f32[24,512]{1,0:T(8,128)S(1)} %copy-done), channel_id=1, source_target_pairs={{1,0},{2,1},{3,2},{4,3},{5,4},{6,5},{7,6},{8,7},{9,8},{10,9},{11,1... | collective-permute-start | bytes 147464 | tf_op jit(solution)/shard_map/ppermute | solution.py:17
